TPU v7x, 512 devices: a whole 4x4x16 slice. The times are simulated.
512 devices in a mesh: gx: 16 (over y, z_hi, core), gy: 32 (over z_lo, x).
Axes of the slice: x: 4, y: 4, z: 16 (z_hi: 2, z_lo: 8; z = z_hi * 8 + z_lo), core: 2. Of those that a mesh axis runs over, the one named last changes fastest.
Arguments:
- layer_input: bfloat16 [16384, 2048], P('gy', 'gx'), may hold values from -6 to 6
- project_weight: bfloat16 [2048, 3, 2048], P(None, None, 'gx'), may hold values from -0.125 to 0.125
- output_weight: bfloat16 [2048, 2048], P('gx'), may hold values from -0.5 to 0.5
- cache_entries: bfloat16 [32, 3584, 2, 2048], P('gy', None, None, 'gx'), may hold values from -400 to 400, as said below
- cached_lengths: int32 [32], replicated, may hold values from 1 to 3584, as said below
- final_gain: bfloat16 [2048], P('gx'), may hold values from 0.099609375 to 1.8984375
- head_weight: bfloat16 [76032, 2048], P('gy', 'gx'), may hold values from -0.125 to 0.125
Outputs:
- layer_output: bfloat16 [16384, 2048], P('gy', 'gx')
- appended_entries: bfloat16 [16384, 2, 2048], P('gy', None, 'gx')
- logit_scale: float32 [32], P('gx')
- logit_peak: float32 [32], P('gx')
Inputs may be any that keep to these rules, and one draw needn't show every extreme that they name: `cached_lengths`: every request has one cached slot or more; in every draw one request uses all 3584 slots and another exactly one. `cache_entries`: slots at or beyond a request's cached length are never read.
All inputs are finite; a program needn't handle non-finite values.
Results may differ from a plain program's by a relative error of at most 0.015.
Values may be sent and summed in bfloat16 or wider, within the bound.
No kernel may reach another device: no remote copies, remote signals or barrier semaphores. Data moves between devices by JAX's collectives and lax.ppermute only.
A program may use at most 64 MiB of HBM per device.

v0:
```python
import jax
import jax.numpy as jnp
from jax import lax
from jax.sharding import PartitionSpec as P

D = 2048
HEAD_DIM = 128
VOCAB = 76032
NEG_FILL = -1e30


def combined_all(part, axis, combine):
    gathered = jax.tree.map(lambda a: lax.all_gather(a, axis), part)

    def take(source):
        return jax.tree.map(lambda a: lax.dynamic_index_in_dim(a, source, 0, False), gathered)

    return lax.fori_loop(
        1, lax.axis_size(axis), lambda source, state: combine(state, take(source)), take(0)
    )


def fold_scores(carried, queries, key_block, value_block, allowed):
    running_max, mass_sum, weighted = carried
    scores = jnp.einsum(
        "qhd,khd->hqk", queries, key_block, preferred_element_type=jnp.float32
    ) * HEAD_DIM ** (-0.5)
    scores = jnp.where(allowed, scores, NEG_FILL)
    new_max = jnp.maximum(running_max, jnp.max(scores, axis=2))
    weights = jnp.where(allowed, jnp.exp(scores - new_max[:, :, None]), 0.0)
    factor = jnp.exp(running_max - new_max)
    mass_sum = mass_sum * factor + jnp.sum(weights, axis=2)
    weighted = weighted * factor[:, :, None] + jnp.einsum(
        "hqk,khd->hqd", weights, value_block.astype(jnp.float32), precision=lax.Precision.HIGHEST
    )
    return (new_max, mass_sum, weighted)


def cache_pass(queries, cache_part, live_slots, block_rows):
    query_rows, head_count, head_width = queries.shape
    block_count = cache_part.shape[0] // block_rows
    live_slots = jnp.clip(live_slots, 0, cache_part.shape[0])
    initial = (
        jnp.full((head_count, query_rows), NEG_FILL, jnp.float32),
        jnp.zeros((head_count, query_rows), jnp.float32),
        jnp.zeros((head_count, query_rows, head_width), jnp.float32),
    )

    def advance(block_index, carried):
        cache_piece = lax.dynamic_slice_in_dim(cache_part, block_index * block_rows, block_rows, 0)
        key_block = cache_piece[:, 0].reshape(block_rows, head_count, head_width)
        value_block = cache_piece[:, 1].reshape(block_rows, head_count, head_width)
        places = block_index * block_rows + jnp.arange(block_rows, dtype=jnp.int32)
        allowed = (places < live_slots)[None, None, :]
        return fold_scores(carried, queries, key_block, value_block, allowed)

    return lax.fori_loop(0, block_count, advance, initial)


def combine_stats(earlier, other_side):
    return (earlier[0] + other_side[0], jnp.maximum(earlier[1], other_side[1]))


def per_device(
    layer_input,
    project_weight,
    output_weight,
    cache_entries,
    cached_lengths,
    final_gain,
    head_weight,
):
    new_rows = layer_input.shape[0]
    head_count = output_weight.shape[0] // HEAD_DIM
    request = lax.axis_index("gy")
    own_len = lax.dynamic_index_in_dim(cached_lengths, request, 0, keepdims=False)
    features = lax.all_gather(layer_input, "gx", axis=1, tiled=True)
    widened = features.astype(jnp.float32)
    normed = (
        widened * lax.rsqrt(jnp.mean(widened * widened, axis=1, keepdims=True) + 1e-06)
    ).astype(jnp.bfloat16)
    projected = jnp.einsum(
        "td,dcf->tcf", normed, project_weight, preferred_element_type=jnp.float32
    )
    rounded = projected.astype(jnp.bfloat16)
    queries = rounded[:, 0].reshape(new_rows, head_count, HEAD_DIM)
    new_keys = rounded[:, 1].reshape(new_rows, head_count, HEAD_DIM)
    new_values = rounded[:, 2].reshape(new_rows, head_count, HEAD_DIM)
    appended = rounded[:, 1:3]
    cache_local = cache_entries[0]
    cache_slots = cache_local.shape[0]
    block_rows = min(256, cache_slots // 2)
    carried = cache_pass(queries, cache_local, own_len, block_rows)
    causal = (jnp.arange(new_rows)[None, :] <= jnp.arange(new_rows)[:, None])[None]
    carried = fold_scores(carried, queries, new_keys, new_values, causal)
    attended = (carried[2] / carried[1][:, :, None]).astype(jnp.bfloat16)
    attended = jnp.transpose(attended, (1, 0, 2)).reshape(new_rows, head_count * HEAD_DIM)
    partial_out = jnp.dot(attended, output_weight, preferred_element_type=jnp.float32)
    branch_sum = lax.psum_scatter(
        partial_out.astype(jnp.bfloat16), "gx", scatter_dimension=1, tiled=True
    ).astype(jnp.float32)
    layer_output = (layer_input.astype(jnp.float32) + branch_sum).astype(jnp.bfloat16)
    last_row = layer_output[new_rows - 1 :]
    every_last = lax.all_gather(last_row, "gy", axis=0, tiled=True)
    last_wide = every_last.astype(jnp.float32)
    square_part = jnp.sum(last_wide * last_wide, axis=1)
    gained = (last_wide * final_gain.astype(jnp.float32)).astype(jnp.bfloat16)
    logit_part = jnp.einsum("rd,vd->rv", gained, head_weight, preferred_element_type=jnp.float32)
    logit_rows, square_rows = (
        lax.psum_scatter(logit_part, "gx", scatter_dimension=0, tiled=True),
        lax.psum_scatter(square_part, "gx", scatter_dimension=0, tiled=True),
    )
    logits = logit_rows * lax.rsqrt(square_rows / D + 1e-06)[:, None]
    square_sums = jnp.sum(logits * logits, axis=1)
    row_peaks = jnp.max(logits, axis=1)
    total_squares, logit_peak = combined_all((square_sums, row_peaks), "gy", combine_stats)
    logit_scale = jnp.sqrt(total_squares / VOCAB)
    return (layer_output, appended, logit_scale, logit_peak)


def solution(mesh):
    return jax.shard_map(
        per_device,
        mesh=mesh,
        in_specs=(
            P("gy", "gx"),
            P(None, None, "gx"),
            P("gx", None),
            P("gy", None, None, "gx"),
            P(),
            P("gx"),
            P("gy", "gx"),
        ),
        out_specs=(P("gy", "gx"), P("gy", None, "gx"), P("gx"), P("gx")),
        check_vma=False,
    )
```

profile of v0, /device:TPU:0, one launch (start us, length us, event | category | flops | bytes accessed | tf_op | source)
XLA Modules:
  0.0 776.4 jit_solution(6854591349324929596)
XLA Ops:
  8.0 3.0 copy.20
  12.2 88.2 %all-gather.5.cloned.1.call-done = bf16[512,2048]{1,0:T(8,128)(2,1)} async-done(((bf16[512,128]{1,0:T(8,128)(2,1)}), bf16[512,2048]{1,0:T(8,128)(2,1)}) %all-gather.5.cloned.1.call-update) | async-done | bytes 2097168 | tf_op jit(solution)/shard_map/all_gather | solution.py:77
  100.4 2.2 fusion.13
  102.6 1.3 fusion.20
  104.9 57.1 %while.36 = (s32[]{:T(128)}, f32[1,512]{1,0:T(1,128)S(1)}, f32[1,512]{1,0:T(1,128)}, f32[1,512,128]{2,1,0:T(8,128)S(1)}, s32[]{:T(128)}, /*index=5*/bf16[3584,2,...) while((s32[]{:T(128)}, f32[1,512]{1,0:T(1,128)S(1)}, ...), condition=%wide.region_4.5_spmd.clone, body=%wide.region_1.4_spmd.clone.sunk | while | flops 236129280 | bytes 2393295 | solution.py:57
  106.7 1.6 fusion.53
  109.6 1.3 fusion.52
  110.8 1.6 fusion.53
  112.5 1.1 fusion.49
  113.7 1.3 fusion.52
  115.0 1.6 fusion.53
  116.6 1.1 fusion.49
  117.8 1.3 fusion.52
  119.1 1.6 fusion.53
  122.0 1.3 fusion.52
  123.2 1.6 fusion.53
  126.1 1.3 fusion.52
  127.4 1.6 fusion.53
  129.0 1.1 fusion.49
  130.2 1.3 fusion.52
  131.5 1.6 fusion.53
  134.4 1.3 fusion.52
  135.6 1.6 fusion.53
  137.2 1.1 fusion.49
  138.5 1.3 fusion.52
  139.8 1.6 fusion.53
  142.6 1.3 fusion.52
  143.9 1.6 fusion.53
  146.7 1.3 fusion.52
  148.0 1.6 fusion.53
  150.9 1.3 fusion.52
  152.2 1.6 fusion.53
  155.0 1.3 fusion.52
  156.3 1.6 fusion.53
  159.1 1.3 fusion.52
  160.4 1.6 fusion.53
  163.6 1.7 fusion.26
  165.3 2.0 convolution_convert_fusion
  167.3 3.9 copy.17
  171.9 112.6 %reduce-scatter.4.cloned.1.call-done = bf16[128,512]{1,0:T(8,128)(2,1)} async-done(((bf16[2048,512]{1,0:T(8,128)(2,1)}), bf16[128,512]{1,0:T(8,128)(2,1)}) %reduce-scatter.4.cloned.1.call-update) | async-done | bytes 131088
  285.7 112.4 %all-gather.2 = bf16[32,1,128]{2,1,0:T(2,128)(2,1)S(1)} all-gather(bf16[1,1,128]{2,1,0:T(2,128)(2,1)S(1)} %slice_bitcast_fusion.4), channel_id=1, replica_groups=mesh['gx'=16,'gy'=32] {'gy'}, dimensions={0}, use_global_device_ids=true | all-gather | bytes 8448 | tf_op jit(solution)/shard_map/all_gather | solution.py:104
  399.1 1.3 dynamic-slice.2
  401.1 1.3 dynamic-slice
  404.1 62.1 %all-reduce.3 = f32[32]{0:T(128)S(1)} all-reduce(f32[32]{0:T(128)S(1)} %multiply_reduce_fusion.1), channel_id=6, replica_groups=mesh['gx'=16,'gy'=32] {'gx'}, use_global_device_ids=true, to_apply=%region_10.11.clone | all-reduce | flops 32 | bytes 256
  466.2 177.4 %all-reduce.7.cloned.1.call-done = f32[32,2376]{1,0:T(8,128)} async-done(((f32[32,2376]{1,0:T(8,128)}), f32[32,2376]{1,0:T(8,128)}) %all-reduce.7.cloned.1.call-update) | async-done | bytes 304144
  643.7 1.1 fusion.31
  645.3 122.6 %all-reduce.4 = (f32[64]{0:T(128)S(1)}, f32[64]{0:T(128)S(1)}) all-reduce(f32[64]{0:T(128)S(1)} %dynamic-update-slice, f32[64]{0:T(128)S(1)} %dynamic-update-slice.1), channel_id=2, replica_groups=mesh['gx'=16,'gy'=32] {'gy'}, use_global_device_ids=true, to_apply=%add | all-reduce | flops 128 | bytes 1024
  768.0 1.3 while.35
  (152 shorter events, 23.0 us)
Async XLA Ops:
  7.2 95.5 %copy-start = (bf16[2048,3,128]{2,0,1:T(8,128)(2,1)S(1)}, bf16[2048,3,128]{2,0,1:T(8,128)(2,1)}, u32[]{:S(2)}) copy-start(bf16[2048,3,128]{2,0,1:T(8,128)(2,1)} %param.12) | copy-start | bytes 4718596
  7.2 3.8 copy-start.8
  7.2 93.2 %all-gather.5.cloned.1.call-start = ((), (), s32[]{:S(2)}) async-start(), calls=%async_computation.1 | async-start | bytes 2228224 | tf_op jit(solution)/shard_map/all_gather | solution.py:77
  7.9 276.6 %reduce-scatter.4.cloned.1.call-start = ((), (), s32[]{:S(2)}) async-start(), calls=%async_computation.2 | async-start | bytes 2228224
  100.4 2.2 copy-start.1
  103.9 0.9 copy-start.2
  162.0 3.3 copy-start.5
  171.2 0.7 copy-start.9
  171.2 114.3 %copy-start.4 = (bf16[512,128]{1,0:T(8,128)(2,1)S(1)}, bf16[512,128]{1,0:T(8,128)(2,1)}, u32[]{:S(2)}) copy-start(bf16[512,128]{1,0:T(8,128)(2,1)} %param.11) | copy-start | bytes 393220
  171.2 226.8 %copy-start.3 = (bf16[2376,128]{1,0:T(8,128)(2,1)S(1)}, bf16[2376,128]{1,0:T(8,128)(2,1)}, u32[]{:S(2)}) copy-start(bf16[2376,128]{1,0:T(8,128)(2,1)} %param.17) | copy-start | bytes 1824772
  171.2 231.7 %slice-start = ((bf16[512,3,128]{2,0,1:T(8,128)(2,1)}), bf16[512,2,128]{2,0,1:T(8,128)(2,1)S(1)}, s32[]{:S(2)}) async-start(bf16[512,3,128]{2,0,1:T(8,128)(2,1)} %copy-done.2), calls=%async_computation.4 | async-start | bytes 524288 | tf_op jit(solution)/shard_map/slice | solution.py:89
  171.3 472.4 %all-reduce.7.cloned.1.call-start = ((), (), s32[]{:S(2)}) async-start(), calls=%async_computation.3 | async-start | bytes 622592
  285.6 484.3 %copy-start.6 = (bf16[512,128]{1,0:T(8,128)(2,1)}, bf16[512,128]{1,0:T(8,128)(2,1)S(1)}, u32[]{:S(2)}) copy-start(bf16[512,128]{1,0:T(8,128)(2,1)S(1)} %add_convert_fusion) | copy-start | bytes 393220
  769.4 0.5 copy-start.7
Sparse Core Ops, SparseCore 0:
  11.2 89.1 all-gather.4
  171.4 113.0 reduce-scatter.3
  399.2 244.3 all-reduce.6
where the time goes:
time: 778 us; the launch traced here: 776 us
  waiting for transfers between devices  379 us (49%)
  blocking collectives  297 us (38%)
  matrix products  44 us (6%)
  other arithmetic  25.5 us (3%)
  between operations  15.9 us (2%)
  local copies, waits for them, and re-layouts  13.4 us (2%)
    unnamed x5, waiting for transfers between devices  291 us
    unnamed x2, blocking collectives  185 us
    all_gather x1, blocking collectives, per_device(): every_last = lax.all_gather(last_row, 'gy', axis=0, tiled=True)  112 us
    all_gather x1, waiting for transfers between devices, per_device(): features = lax.all_gather(layer_input, 'gx', axis=1, tiled=True)  88.2 us
    dot_general x15, matrix products, fold_scores(): jnp.einsum('hqk,khd->hqd', weights, value_block.astype(jnp.float32), prec...  23.6 us
    add x15, other arithmetic, fold_scores(): mass_sum = mass_sum * factor + jnp.sum(weights, axis=2)  17.9 us
    dot_general x15, matrix products, fold_scores(): jnp.einsum('qhd,khd->hqk', queries, key_block, preferred_element_type=jnp...  16.1 us
  transfers between devices with their start and end apart: 3, of which 3 were waited for; matrix products, arithmetic and copies ran while one was open for 1% of the time, Pallas kernels for 0%

commit v1 on v0

--- a/solution.py
+++ b/solution.py
@@ -101,7 +101,9 @@
     ).astype(jnp.float32)
     layer_output = (layer_input.astype(jnp.float32) + branch_sum).astype(jnp.bfloat16)
     last_row = layer_output[new_rows - 1 :]
-    every_last = lax.all_gather(last_row, "gy", axis=0, tiled=True)
+    every_last = jnp.concatenate(
+        lax.all_to_all(jnp.stack([last_row] * lax.axis_size("gy")), "gy", 0, 0), axis=0
+    )
     last_wide = every_last.astype(jnp.float32)
     square_part = jnp.sum(last_wide * last_wide, axis=1)
     gained = (last_wide * final_gain.astype(jnp.float32)).astype(jnp.bfloat16)

time: 778 us -> 686 us (0.88)
  blocking collectives: 297 us -> 189 us
  waiting for transfers between devices: 379 us -> 389 us
    all_gather x1 -> x0, blocking collectives: 112 us -> none  [per_device(): every_last = lax.all_gather(last_row, 'gy', axis=0, tiled=True)]
    all_to_all x0 -> x1, waiting for transfers between devices: none -> 12.4 us  [per_device(): lax.all_to_all(jnp.stack([last_row] * lax.axis_size('gy')), 'gy', 0, 0)]
  transfers between devices with their start and end apart: 3 -> 4, of which waited for: 3 -> 4; matrix products, arithmetic and copies ran while one was open for 1% -> 1% of each run, Pallas kernels for 0% -> 0%
where the time goes in v1:
time: 686 us; the launch traced here: 684 us
  waiting for transfers between devices  389 us (57%)
  blocking collectives  189 us (28%)
  matrix products  44 us (6%)
  other arithmetic  25.5 us (4%)
  between operations  16 us (2%)
  local copies, waits for them, and re-layouts  13.4 us (2%)
    unnamed x5, waiting for transfers between devices  289 us
    unnamed x2, blocking collectives  189 us
    all_gather x1, waiting for transfers between devices, per_device(): features = lax.all_gather(layer_input, 'gx', axis=1, tiled=True)  88.2 us
    dot_general x15, matrix products, fold_scores(): jnp.einsum('hqk,khd->hqd', weights, value_block.astype(jnp.float32), prec...  23.6 us
    add x15, other arithmetic, fold_scores(): mass_sum = mass_sum * factor + jnp.sum(weights, axis=2)  17.9 us
    dot_general x15, matrix products, fold_scores(): jnp.einsum('qhd,khd->hqk', queries, key_block, preferred_element_type=jnp...  16.1 us
  transfers between devices with their start and end apart: 4, of which 4 were waited for; matrix products, arithmetic and copies ran while one was open for 1% of the time, Pallas kernels for 0%

profile of v1, /device:TPU:0, one launch (start us, length us, event | category | flops | bytes accessed | tf_op | source)
XLA Modules:
  0.0 683.8 jit_solution(18303286564782547247)
XLA Ops:
  8.0 3.0 copy.24
  12.2 88.2 %all-gather.4.cloned.1.call-done = bf16[512,2048]{1,0:T(8,128)(2,1)} async-done(((bf16[512,128]{1,0:T(8,128)(2,1)}), bf16[512,2048]{1,0:T(8,128)(2,1)}) %all-gather.4.cloned.1.call-update) | async-done | bytes 2097168 | tf_op jit(solution)/shard_map/all_gather | solution.py:77
  100.4 2.2 fusion.13
  102.6 1.3 fusion.20
  104.9 57.1 %while.36 = (s32[]{:T(128)}, f32[1,512]{1,0:T(1,128)S(1)}, f32[1,512]{1,0:T(1,128)}, f32[1,512,128]{2,1,0:T(8,128)S(1)}, s32[]{:T(128)}, /*index=5*/bf16[3584,2,...) while((s32[]{:T(128)}, f32[1,512]{1,0:T(1,128)S(1)}, ...), condition=%wide.region_4.5_spmd.clone, body=%wide.region_1.4_spmd.clone.sunk | while | flops 236129280 | bytes 2393295 | solution.py:57
  106.7 1.6 fusion.53
  109.6 1.3 fusion.52
  110.8 1.6 fusion.53
  112.5 1.1 fusion.49
  113.7 1.3 fusion.52
  115.0 1.6 fusion.53
  116.6 1.1 fusion.49
  117.8 1.3 fusion.52
  119.1 1.6 fusion.53
  122.0 1.3 fusion.52
  123.2 1.6 fusion.53
  126.1 1.3 fusion.52
  127.4 1.6 fusion.53
  129.0 1.1 fusion.49
  130.2 1.3 fusion.52
  131.5 1.6 fusion.53
  134.4 1.3 fusion.52
  135.6 1.6 fusion.53
  138.5 1.3 fusion.52
  139.8 1.6 fusion.53
  142.6 1.3 fusion.52
  143.9 1.6 fusion.53
  146.7 1.3 fusion.52
  148.0 1.6 fusion.53
  150.9 1.3 fusion.52
  152.2 1.6 fusion.53
  155.0 1.3 fusion.52
  156.3 1.6 fusion.53
  159.1 1.3 fusion.52
  160.4 1.6 fusion.53
  163.6 1.7 fusion.26
  165.3 2.0 convolution_convert_fusion
  167.3 3.9 copy.21
  171.3 113.3 %reduce-scatter.4.cloned.1.call-done = bf16[128,512]{1,0:T(8,128)(2,1)} async-done(((bf16[2048,512]{1,0:T(8,128)(2,1)}), bf16[128,512]{1,0:T(8,128)(2,1)}) %reduce-scatter.4.cloned.1.call-update) | async-done | bytes 131088
  286.3 4.9 all-to-all-start
  291.3 12.4 %all-to-all-done = bf16[32,1,128]{2,1,0:T(2,128)(2,1)S(1)} async-done(((bf16[32,1,128]{2,1,0:T(2,128)(2,1)}), bf16[32,1,128]{2,1,0:T(2,128)(2,1)S(1)}, u32[]{:S(2)}, u32[]{:S(2)}) %all-to-all-start) | async-done | bytes 8224 | tf_op jit(solution)/shard_map/all_to_all | solution.py:105
  304.8 1.3 dynamic-slice.2
  306.7 1.3 dynamic-slice
  309.7 66.6 %all-reduce.3 = f32[32]{0:T(128)S(1)} all-reduce(f32[32]{0:T(128)S(1)} %multiply_reduce_fusion.1), channel_id=6, replica_groups=mesh['gx'=16,'gy'=32] {'gx'}, use_global_device_ids=true, to_apply=%region_10.11.clone | all-reduce | flops 32 | bytes 256
  376.4 174.6 %all-reduce.7.cloned.1.call-done = f32[32,2376]{1,0:T(8,128)} async-done(((f32[32,2376]{1,0:T(8,128)}), f32[32,2376]{1,0:T(8,128)}) %all-reduce.7.cloned.1.call-update) | async-done | bytes 304144
  551.1 1.1 fusion.31
  552.6 122.6 %all-reduce.4 = (f32[64]{0:T(128)S(1)}, f32[64]{0:T(128)S(1)}) all-reduce(f32[64]{0:T(128)S(1)} %dynamic-update-slice, f32[64]{0:T(128)S(1)} %dynamic-update-slice.1), channel_id=2, replica_groups=mesh['gx'=16,'gy'=32] {'gy'}, use_global_device_ids=true, to_apply=%add | all-reduce | flops 128 | bytes 1024
  675.4 1.3 while.35
  (154 shorter events, 24.2 us)
Async XLA Ops:
  7.2 95.5 %copy-start = (bf16[2048,3,128]{2,0,1:T(8,128)(2,1)S(1)}, bf16[2048,3,128]{2,0,1:T(8,128)(2,1)}, u32[]{:S(2)}) copy-start(bf16[2048,3,128]{2,0,1:T(8,128)(2,1)} %param.12) | copy-start | bytes 4718596
  7.2 3.8 copy-start.8
  7.2 93.2 %all-gather.4.cloned.1.call-start = ((), (), s32[]{:S(2)}) async-start(), calls=%async_computation.2 | async-start | bytes 2228224 | tf_op jit(solution)/shard_map/all_gather | solution.py:77
  7.9 276.6 %reduce-scatter.4.cloned.1.call-start = ((), (), s32[]{:S(2)}) async-start(), calls=%async_computation.3 | async-start | bytes 2228224
  100.4 2.2 copy-start.1
  103.9 0.9 copy-start.2
  162.0 3.3 copy-start.5
  171.2 114.3 %copy-start.4 = (bf16[512,128]{1,0:T(8,128)(2,1)S(1)}, bf16[512,128]{1,0:T(8,128)(2,1)}, u32[]{:S(2)}) copy-start(bf16[512,128]{1,0:T(8,128)(2,1)} %param.11) | copy-start | bytes 393220
  171.2 120.0 %copy-start.9 = (bf16[128]{0:T(256)(128)(2,1)S(1)}, bf16[128]{0:T(256)(128)(2,1)}, u32[]{:S(2)}) copy-start(bf16[128]{0:T(256)(128)(2,1)} %param.16) | copy-start | bytes 772
  171.2 132.5 %copy-start.3 = (bf16[2376,128]{1,0:T(8,128)(2,1)S(1)}, bf16[2376,128]{1,0:T(8,128)(2,1)}, u32[]{:S(2)}) copy-start(bf16[2376,128]{1,0:T(8,128)(2,1)} %param.17) | copy-start | bytes 1824772
  171.2 137.4 %slice-start = ((bf16[512,3,128]{2,0,1:T(8,128)(2,1)}), bf16[512,2,128]{2,0,1:T(8,128)(2,1)S(1)}, s32[]{:S(2)}) async-start(bf16[512,3,128]{2,0,1:T(8,128)(2,1)} %copy-done.2), calls=%async_computation.5 | async-start | bytes 524288 | tf_op jit(solution)/shard_map/slice | solution.py:89
  285.6 391.6 %copy-start.6 = (bf16[512,128]{1,0:T(8,128)(2,1)}, bf16[512,128]{1,0:T(8,128)(2,1)S(1)}, u32[]{:S(2)}) copy-start(bf16[512,128]{1,0:T(8,128)(2,1)S(1)} %add_convert_fusion) | copy-start | bytes 393220
  286.3 17.4 %all-to-all-start = ((bf16[32,1,128]{2,1,0:T(2,128)(2,1)}), bf16[32,1,128]{2,1,0:T(2,128)(2,1)S(1)}, u32[]{:S(2)}, u32[]{:S(2)}) async-start(bf16[32,1,128]{2,1,0:T(2,128)(2,1)} %stack.2), calls=%async_computation | async-start | bytes 32768 | tf_op jit(solution)/shard_map/all_to_all | solution.py:105
  291.2 259.9 %all-reduce.7.cloned.1.call-start = ((), (), s32[]{:S(2)}) async-start(), calls=%async_computation.4 | async-start | bytes 622592
  676.7 0.5 copy-start.7
Sparse Core Ops, SparseCore 0:
  11.2 89.1 all-gather.3
  171.4 113.0 reduce-scatter.3
  304.9 246.1 all-reduce.6
